TPU v7x, 128 devices: a whole 4x4x4 slice. The times are simulated.
128 devices in a mesh: dp: 32 (over x, y, core), tensor: 4 (over z).
Axes of the slice: x: 4, y: 4, z: 4, core: 2. Of those that a mesh axis runs over, the one named last changes fastest.
Arguments:
- query: bfloat16 [32768, 5120], P('dp', 'tensor'), may hold values from -6 to 6
- keys: bfloat16 [32768, 1024], P('dp', 'tensor'), may hold values from -6 to 6
- values: bfloat16 [32768, 1024], P('dp', 'tensor'), may hold values from -6 to 6
- out_weight: bfloat16 [5120, 2560], P('tensor', 'dp'), may hold values from -0.078125 to 0.078125
- loss_grad: bfloat16 [32768, 2560], P('dp', 'tensor'), may hold values from -6 to 6
- lengths: int32 [32, 16], P('dp'), may hold values from 1 to 512, 1024 in all within a row
- languages: int32 [32, 16], P('dp'), may hold values from 0 to 28
- labels: int32 [32768], P('dp'), may hold values from -100 to 152063, as said below
Outputs:
- attention_result: bfloat16 [32768, 5120], P('dp', 'tensor')
- query_gradient: bfloat16 [32768, 5120], P('dp', 'tensor')
- key_gradient: bfloat16 [32768, 1024], P('dp', 'tensor')
- value_gradient: bfloat16 [32768, 1024], P('dp', 'tensor')
- projection_gradient: bfloat16 [5120, 2560], P('tensor')
Inputs may be any that keep to these rules, and one draw needn't show every extreme that they name: `labels`: each label is -100, meaning no loss on that token, or a token id below 152064.
All inputs are finite; a program needn't handle non-finite values.
Results may differ from a plain program's by a relative error of at most 0.02.
Values may be sent and summed in bfloat16 or wider, within the bound.
No kernel may reach another device: no remote copies, remote signals or barrier semaphores. Data moves between devices by JAX's collectives and lax.ppermute only.
A program may use at most 192 MiB of HBM per device.

v0:
```python
import functools
import math

import jax
import jax.numpy as jnp
from jax import lax
from jax.experimental import pallas as pl
from jax.experimental.pallas import tpu as pltpu
from jax.sharding import PartitionSpec as P


QUERY_HEADS = 40
KEY_VALUE_HEADS = 8
HEAD_SIZE = 128
LANGS = 29
DOCS = 16
COUNT_BASE = 32


def token_docs(length_row, row_count):
    doc_ends = jnp.cumsum(length_row)
    places = jnp.arange(row_count, dtype=jnp.int32)
    return jnp.sum((places[:, None] >= doc_ends[None, :]).astype(jnp.int32), axis=1)


GROUP = QUERY_HEADS // KEY_VALUE_HEADS
ROW_BLOCK = 256
MASKED = -1e30
NT_DIMS = (((1,), (1,)), ((), ()))


def block_mask(row_doc_ref, col_doc_ref, first_row, key_end):
    row_doc = row_doc_ref[first_row : first_row + ROW_BLOCK, :]
    col_doc = col_doc_ref[:, :key_end]
    shape = (ROW_BLOCK, key_end)
    rows = lax.broadcasted_iota(jnp.int32, shape, 0) + first_row
    cols = lax.broadcasted_iota(jnp.int32, shape, 1)
    return (row_doc == col_doc) & (cols <= rows)


def forward_kernel(factor, q_ref, k_ref, v_ref, row_doc_ref, col_doc_ref, o_ref, lse_ref):
    row_count = q_ref.shape[0]
    for block in range(row_count // ROW_BLOCK):
        first_row = block * ROW_BLOCK
        key_end = first_row + ROW_BLOCK
        allowed = block_mask(row_doc_ref, col_doc_ref, first_row, key_end)
        rows = pl.ds(first_row, ROW_BLOCK)

        def head_body(head, carry):
            cols = pl.ds(pl.multiple_of(head * HEAD_SIZE, HEAD_SIZE), HEAD_SIZE)
            query = q_ref[rows, cols]
            scores = lax.dot_general(
                query, k_ref[:key_end, :], NT_DIMS, preferred_element_type=jnp.float32
            ) * factor
            scores = jnp.where(allowed, scores, MASKED)
            top = jnp.max(scores, axis=1, keepdims=True)
            log_total = top + jnp.log(jnp.sum(jnp.exp(scores - top), axis=1, keepdims=True))
            weights = jnp.exp(scores - log_total).astype(jnp.bfloat16)
            result = jnp.dot(weights, v_ref[:key_end, :], preferred_element_type=jnp.float32)
            o_ref[rows, cols] = result.astype(o_ref.dtype)
            lse_ref[0, head, rows, :] = jnp.broadcast_to(log_total, (ROW_BLOCK, HEAD_SIZE))
            return carry

        lax.fori_loop(0, GROUP, head_body, 0)


def backward_kernel(
    factor, q_ref, k_ref, v_ref, row_doc_ref, col_doc_ref, o_ref, do_ref, lse_ref,
    dq_ref, dk_ref, dv_ref, dk_acc, dv_acc,
):
    row_count = q_ref.shape[0]
    dk_acc[...] = jnp.zeros_like(dk_acc)
    dv_acc[...] = jnp.zeros_like(dv_acc)
    for block in range(row_count // ROW_BLOCK):
        first_row = block * ROW_BLOCK
        key_end = first_row + ROW_BLOCK
        allowed = block_mask(row_doc_ref, col_doc_ref, first_row, key_end)
        rows = pl.ds(first_row, ROW_BLOCK)

        def head_body(head, carry):
            cols = pl.ds(pl.multiple_of(head * HEAD_SIZE, HEAD_SIZE), HEAD_SIZE)
            query = q_ref[rows, cols]
            grad = do_ref[rows, cols]
            keys = k_ref[:key_end, :]
            values = v_ref[:key_end, :]
            log_total = lse_ref[0, head, rows, :][:, :1]
            scores = lax.dot_general(query, keys, NT_DIMS, preferred_element_type=jnp.float32) * factor
            scores = jnp.where(allowed, scores, MASKED)
            weights = jnp.exp(scores - log_total)
            dv_acc[:key_end, :] += jnp.dot(
                weights.astype(jnp.bfloat16).T, grad, preferred_element_type=jnp.float32
            )
            weight_grad = lax.dot_general(grad, values, NT_DIMS, preferred_element_type=jnp.float32)
            diagonal = jnp.sum(
                grad.astype(jnp.float32) * o_ref[rows, cols].astype(jnp.float32), axis=1, keepdims=True
            )
            score_grad = (weights * (weight_grad - diagonal) * factor).astype(jnp.bfloat16)
            dq_ref[rows, cols] = jnp.dot(score_grad, keys, preferred_element_type=jnp.float32).astype(
                dq_ref.dtype
            )
            dk_acc[:key_end, :] += jnp.dot(score_grad.T, query, preferred_element_type=jnp.float32)
            return carry

        lax.fori_loop(0, GROUP, head_body, 0)
    dk_ref[...] = dk_acc[...].astype(dk_ref.dtype)
    dv_ref[...] = dv_acc[...].astype(dv_ref.dtype)


def doc_views(doc_ids):
    return doc_ids[:, None], doc_ids[None, :]


def attention_forward(query, keys, values, doc_ids, factor):
    row_count = query.shape[0]
    groups = keys.shape[1] // HEAD_SIZE
    width = GROUP * HEAD_SIZE
    row_doc, col_doc = doc_views(doc_ids)
    flops = 4 * groups * GROUP * row_count * row_count * HEAD_SIZE
    return pl.pallas_call(
        functools.partial(forward_kernel, factor),
        grid=(groups,),
        in_specs=[
            pl.BlockSpec((row_count, width), lambda g: (0, g)),
            pl.BlockSpec((row_count, HEAD_SIZE), lambda g: (0, g)),
            pl.BlockSpec((row_count, HEAD_SIZE), lambda g: (0, g)),
            pl.BlockSpec((row_count, 1), lambda g: (0, 0)),
            pl.BlockSpec((1, row_count), lambda g: (0, 0)),
        ],
        out_specs=[
            pl.BlockSpec((row_count, width), lambda g: (0, g)),
            pl.BlockSpec((1, GROUP, row_count, HEAD_SIZE), lambda g: (g, 0, 0, 0)),
        ],
        out_shape=[
            jax.ShapeDtypeStruct(query.shape, query.dtype),
            jax.ShapeDtypeStruct((groups, GROUP, row_count, HEAD_SIZE), jnp.float32),
        ],
        compiler_params=pltpu.CompilerParams(vmem_limit_bytes=48 * 1024 * 1024),
        cost_estimate=pl.CostEstimate(
            flops=flops // 2, transcendentals=groups * GROUP * row_count * row_count // 2,
            bytes_accessed=4 * query.size + 8 * keys.size + 8 * groups * GROUP * row_count * HEAD_SIZE,
        ),
    )(query, keys, values, row_doc, col_doc)


def attention_backward_group(group, query, keys, values, doc_ids, attn, grad, lse, factor):
    row_count = query.shape[0]
    width = GROUP * HEAD_SIZE
    row_doc, col_doc = doc_views(doc_ids)
    flops = 10 * GROUP * row_count * row_count * HEAD_SIZE
    return pl.pallas_call(
        functools.partial(backward_kernel, factor),
        grid=(1,),
        in_specs=[
            pl.BlockSpec((row_count, width), lambda g: (0, group)),
            pl.BlockSpec((row_count, HEAD_SIZE), lambda g: (0, group)),
            pl.BlockSpec((row_count, HEAD_SIZE), lambda g: (0, group)),
            pl.BlockSpec((row_count, 1), lambda g: (0, 0)),
            pl.BlockSpec((1, row_count), lambda g: (0, 0)),
            pl.BlockSpec((row_count, width), lambda g: (0, group)),
            pl.BlockSpec((row_count, width), lambda g: (0, group)),
            pl.BlockSpec((1, GROUP, row_count, HEAD_SIZE), lambda g: (group, 0, 0, 0)),
        ],
        out_specs=[
            pl.BlockSpec((row_count, width), lambda g: (0, 0)),
            pl.BlockSpec((row_count, HEAD_SIZE), lambda g: (0, 0)),
            pl.BlockSpec((row_count, HEAD_SIZE), lambda g: (0, 0)),
        ],
        out_shape=[
            jax.ShapeDtypeStruct((row_count, width), query.dtype),
            jax.ShapeDtypeStruct((row_count, HEAD_SIZE), keys.dtype),
            jax.ShapeDtypeStruct((row_count, HEAD_SIZE), keys.dtype),
        ],
        scratch_shapes=[
            pltpu.VMEM((row_count, HEAD_SIZE), jnp.float32),
            pltpu.VMEM((row_count, HEAD_SIZE), jnp.float32),
        ],
        compiler_params=pltpu.CompilerParams(vmem_limit_bytes=48 * 1024 * 1024),
        cost_estimate=pl.CostEstimate(
            flops=flops // 2, transcendentals=GROUP * row_count * row_count // 2,
            bytes_accessed=2 * 4 * row_count * width + 4 * row_count * HEAD_SIZE * 4
            + 4 * GROUP * row_count * HEAD_SIZE,
        ),
    )(query, keys, values, row_doc, col_doc, attn, grad, lse)


def attach_counts(out_weight, local_counts):
    high = (local_counts // COUNT_BASE).astype(out_weight.dtype)
    low = (local_counts % COUNT_BASE).astype(out_weight.dtype)
    rows = jnp.zeros((16, out_weight.shape[1]), out_weight.dtype)
    rows = rows.at[0, :LANGS].set(high).at[1, :LANGS].set(low)
    return jnp.concatenate([out_weight, rows], axis=0)


def gather_features(block):
    tensor_size = lax.axis_size("tensor")
    me = lax.axis_index("tensor")
    arrived = [block]
    for shift in range(1, tensor_size):
        pairs = [(index, (index + shift) % tensor_size) for index in range(tensor_size)]
        arrived.append(lax.ppermute(block, "tensor", pairs))
    width = block.shape[1]
    full = jnp.zeros((block.shape[0], tensor_size * width), block.dtype)
    for shift, part in enumerate(arrived):
        source = (me - shift) % tensor_size
        full = lax.dynamic_update_slice(full, part, (0, source * width))
    return full


def layer(query, keys, values, out_weight, loss_grad, lengths, languages, labels):
    factor = 1.0 / math.sqrt(HEAD_SIZE)
    row_count = query.shape[0]
    doc_ids = token_docs(lengths[0], row_count).astype(jnp.int32)
    attention_result, log_rows = attention_forward(query, keys, values, doc_ids, factor)
    token_lang = jnp.sum(
        jnp.where(
            doc_ids[:, None] == jnp.arange(DOCS, dtype=jnp.int32)[None, :], languages[0][None, :], 0
        ),
        axis=1,
    )
    counted = labels != -100
    lang_match = token_lang[:, None] == jnp.arange(LANGS, dtype=jnp.int32)[None, :]
    local_counts = jnp.sum((lang_match & counted[:, None]).astype(jnp.int32), axis=0)
    weight_rows = out_weight.shape[0]
    gathered = lax.all_gather(attach_counts(out_weight, local_counts), "dp", axis=1, tiled=True)
    full_weight = gathered[:weight_rows]
    code = gathered[weight_rows : weight_rows + 2].astype(jnp.float32)
    code = code.reshape(2, lax.axis_size("dp"), out_weight.shape[1])[:, :, :LANGS]
    counts = jnp.sum(code[0] * COUNT_BASE + code[1], axis=0)
    lang_weight = jnp.sqrt(jnp.sum(counts) / (LANGS * jnp.maximum(counts, 1.0)))
    token_weight = jnp.where(
        counted, jnp.sum(jnp.where(lang_match, lang_weight[None, :], 0.0), axis=1), 0.0
    )
    full_grad = gather_features(loss_grad)
    weighted = (token_weight[:, None] * full_grad.astype(jnp.float32)).astype(jnp.bfloat16)
    local_term = lax.dot_general(
        attention_result, weighted, (((0,), (0,)), ((), ())), preferred_element_type=jnp.float32
    )
    projection_part = lax.psum_scatter(
        local_term.astype(jnp.bfloat16), "dp", scatter_dimension=0, tiled=True
    )
    projection_gradient = lax.all_gather(projection_part, "dp", axis=0, tiled=True)
    local_term, weighted = lax.optimization_barrier((local_term, weighted))
    out_grad = lax.dot_general(
        weighted,
        full_weight,
        (((1,), (1,)), ((), ())),
        preferred_element_type=jnp.float32,
    ).astype(jnp.bfloat16)

    parts = []
    for group in range(keys.shape[1] // HEAD_SIZE):
        parts.append(
            attention_backward_group(
                group, query, keys, values, doc_ids, attention_result, out_grad, log_rows, factor
            )
        )
    query_gradient, key_gradient, value_gradient = (
        jnp.concatenate([part[k] for part in parts], axis=1) for k in range(3)
    )
    return (attention_result, query_gradient, key_gradient, value_gradient, projection_gradient)


def solution(mesh):
    in_specs = (
        P("dp", "tensor"),
        P("dp", "tensor"),
        P("dp", "tensor"),
        P("tensor", "dp"),
        P("dp", "tensor"),
        P("dp", None),
        P("dp", None),
        P("dp"),
    )
    out_specs = (
        P("dp", "tensor"),
        P("dp", "tensor"),
        P("dp", "tensor"),
        P("dp", "tensor"),
        P("tensor", None),
    )
    return jax.shard_map(layer, mesh=mesh, in_specs=in_specs, out_specs=out_specs, check_vma=False)
```

profile of v0, /device:TPU:0, one launch (start us, length us, event | category | flops | bytes accessed | tf_op | source)
XLA Modules:
  0.0 255.2 jit_solution(10966851012082999114)
XLA Ops:
  7.2 0.8 broadcast_compare_fusion
  10.2 1.6 pad_maximum_fusion.3
  11.9 2.1 collective-permute-start
  14.0 3.6 %collective-permute-start.1 = (bf16[1024,640]{1,0:T(8,128)(2,1)}, bf16[1024,640]{1,0:T(8,128)(2,1)}, u32[]{:S(2)}, u32[]{:S(2)}) collective-permute-start(bf16[1024,640]{1,0:T(8,128)(2,1)} %param.16), channel_id=1, source_target_pairs={{0,2},{1,3},{2,0},{3,1},{4,6},{5,7},{6,4},{7,5},{8,10},{9,11},{10,... | collective-permute-start | bytes 3932168 | tf_op jit(solution)/shard_map/ppermute | solution.py:200
  17.6 1.0 collective-permute-start.2
  18.9 2.7 %broadcast_in_dim.61 = bf16[1024,2560]{1,0:T(8,128)(2,1)} broadcast(bf16[]{:T(256)} %constant.124.clone.1), dimensions={} | broadcast | bytes 5242882 | tf_op jit(solution)/shard_map/broadcast_in_dim | solution.py:202
  21.6 1.2 constant_dynamic-update-slice_fusion.3
  22.8 30.8 %shard_map.119 = (bf16[1024,1280]{1,0:T(8,128)(2,1)}, f32[2,5,1024,128]{3,2,1,0:T(8,128)}) custom-call(bf16[1024,1280]{1,0:T(8,128)(2,1)S(1)} %copy-done, bf16[1024,256]{1,0:T(8,128)(2,1)S(1)} %copy-done.1, bf16[1024,256]{1,0:T(8,128)(2,1)S(1)} %copy-done.3, s32[1024,1]{1,0:T(8,128)S(1)} %copy.21.row_doc_ref, s32[1,1024]{1,0:T(1,128)S(1)} %bitcast.27), custom_call_target="tpu_custom_call" | custom-call | flops 2684354560 | bytes 17825792 | tf_op jit(solution)/shard_map/pallas_call | solution.py:119
  53.6 2.6 %constant_dynamic-update-slice_fusion.2 = bf16[1024,2560]{1,0:T(8,128)(2,1)} fusion(bf16[1024,2560]{1,0:T(8,128)(2,1)} %constant_dynamic-update-slice_fusion.3, bf16[1024,640]{1,0:T(8,128)(2,1)} %collective-permute-done, s32[]{:T(128)S(6)} %select_n.72), kind=kLoop, calls=%fused_computation.29 | loop fusion | bytes 2621444 | tf_op jit(solution)/shard_map/dynamic_update_slice | solution.py:205
  56.2 18.3 %collective-permute-done.1 = bf16[1024,640]{1,0:T(8,128)(2,1)} collective-permute-done((bf16[1024,640]{1,0:T(8,128)(2,1)}, bf16[1024,640]{1,0:T(8,128)(2,1)}, u32[]{:S(2)}, u32[]{:S(2)}) %collective-permute-start.1) | collective-permute-done | bytes 1310752 | tf_op jit(solution)/shard_map/ppermute | solution.py:200
  74.5 2.5 constant_dynamic-update-slice_fusion.1
  77.0 2.5 constant_dynamic-update-slice_fusion
  79.5 1.1 slice.54
  80.7 0.8 fusion.6
  82.3 3.5 %multiply_convert_fusion = bf16[1024,2560]{1,0:T(8,128)(2,1)S(1)} fusion(bf16[1024,2560]{1,0:T(8,128)(2,1)} %constant_dynamic-update-slice_fusion, f32[1024]{0:T(1024)S(1)} %broadcast_select_fusion), kind=kLoop, calls=%fused_computation | loop fusion | flops 7864320 | bytes 10489856 | tf_op jit(solution)/shard_map/convert_element_type | solution.py:234
  85.9 2.3 copy-done.6
  88.2 9.0 %fusion.10 = bf16[1280,2560]{1,0:T(8,128)(2,1)} fusion(bf16[1024,1280]{1,0:T(8,128)(2,1)S(1)} %copy-done.5, bf16[1024,2560]{1,0:T(8,128)(2,1)S(1)} %multiply_convert_fusion), kind=kOutput, calls=%fused_computation.35 | convolution fusion | flops 6710886400 | bytes 14417920 | tf_op jit(solution)/shard_map/dot_general | solution.py:235
  97.4 87.6 %reduce-scatter.2.cloned.1.call-done = bf16[40,2560]{1,0:T(8,128)(2,1)} async-done(((bf16[1280,2560]{1,0:T(8,128)(2,1)}), bf16[40,2560]{1,0:T(8,128)(2,1)}) %reduce-scatter.2.cloned.1.call-update) | async-done | bytes 204816 | tf_op jit(solution)/shard_map/reduce_scatter | solution.py:238
  185.1 11.9 %fusion.2.do_ref = bf16[1024,1280]{1,0:T(8,128)(2,1)} fusion(bf16[1024,2560]{1,0:T(8,128)(2,1)} %copy-done.6, bf16[1296,2560]{0,1:T(8,128)(2,1)} %all-gather.3.cloned.1.call-done), kind=kOutput, calls=%fused_computation.3 | convolution fusion | flops 6712197120 | bytes 14417920 | tf_op jit(solution)/shard_map/dot_general | solution.py:243
  197.0 21.4 %shard_map.121 = (bf16[1024,640]{1,0:T(8,128)(2,1)S(1)}, bf16[1024,128]{1,0:T(8,128)(2,1)S(1)}, bf16[1024,128]{1,0:T(8,128)(2,1)S(1)}) custom-call(bf16[1024,1280]{1,0:T(8,128)(2,1)S(1)} %copy-done, bf16[1024,256]{1,0:T(8,128)(2,1)S(1)} %copy-done.2, bf16[1024,256]{1,0:T(8,128)(2,1)S(1)} %copy-done.4, s32[1024,1]{1,0:T(8,128)S(1)} %copy.21.row_doc_ref, ...), custom_call_target="tpu_custom_call" | custom-call | flops 3355443200 | bytes 9961472 | tf_op jit(solution)/shard_map/pallas_call | solution.py:150
  218.4 21.4 %shard_map.120 = (bf16[1024,640]{1,0:T(8,128)(2,1)S(1)}, bf16[1024,128]{1,0:T(8,128)(2,1)S(1)}, bf16[1024,128]{1,0:T(8,128)(2,1)S(1)}) custom-call(bf16[1024,1280]{1,0:T(8,128)(2,1)S(1)} %copy-done, bf16[1024,256]{1,0:T(8,128)(2,1)S(1)} %copy-done.2, bf16[1024,256]{1,0:T(8,128)(2,1)S(1)} %copy-done.4, s32[1024,1]{1,0:T(8,128)S(1)} %copy.21.row_doc_ref, ...), custom_call_target="tpu_custom_call" | custom-call | flops 3355443200 | bytes 9961472 | tf_op jit(solution)/shard_map/pallas_call | solution.py:150
  239.8 1.1 pad_maximum_fusion.1
  240.9 1.7 pad_maximum_fusion
  242.6 6.1 %copy.31 = bf16[1280,2560]{1,0:T(8,128)(2,1)} copy(bf16[1280,2560]{1,0:T(8,128)(2,1)} %all-gather.5.cloned.1.call-done) | data formatting | bytes 13107200
  (42 shorter events, 3.6 us)
Async XLA Ops:
  7.2 15.6 %copy-start = (bf16[1024,1280]{1,0:T(8,128)(2,1)S(1)}, bf16[1024,1280]{1,0:T(8,128)(2,1)}, u32[]{:S(2)}) copy-start(bf16[1024,1280]{1,0:T(8,128)(2,1)} %q_ref.5) | copy-start | bytes 7864324
  7.2 72.3 %all-gather.3.cloned.1.call-start = ((), (), s32[]{:S(2)}) async-start(), calls=%async_computation.1 | async-start | bytes 7434240 | tf_op jit(solution)/shard_map/all_gather | solution.py:224
  11.9 173.2 %reduce-scatter.2.cloned.1.call-start = ((), (), s32[]{:S(2)}) async-start(), calls=%async_computation.2 | async-start | bytes 6758400 | tf_op jit(solution)/shard_map/reduce_scatter | solution.py:238
  11.9 41.7 %collective-permute-start = (bf16[1024,640]{1,0:T(8,128)(2,1)}, bf16[1024,640]{1,0:T(8,128)(2,1)}, u32[]{:S(2)}, u32[]{:S(2)}) collective-permute-start(bf16[1024,640]{1,0:T(8,128)(2,1)} %param.16), channel_id=1, source_target_pairs={{0,1},{1,2},{2,3},{3,0},{4,5},{5,6},{6,7},{7,4},{8,9},{9,10},{10,1... | collective-permute-start | bytes 3932168 | tf_op jit(solution)/shard_map/ppermute | solution.py:200
  14.0 60.5 %collective-permute-start.1 = (bf16[1024,640]{1,0:T(8,128)(2,1)}, bf16[1024,640]{1,0:T(8,128)(2,1)}, u32[]{:S(2)}, u32[]{:S(2)}) collective-permute-start(bf16[1024,640]{1,0:T(8,128)(2,1)} %param.16), channel_id=1, source_target_pairs={{0,2},{1,3},{2,0},{3,1},{4,6},{5,7},{6,4},{7,5},{8,10},{9,11},{10,... | collective-permute-start | bytes 3932168 | tf_op jit(solution)/shard_map/ppermute | solution.py:200
  17.6 59.4 %collective-permute-start.2 = (bf16[1024,640]{1,0:T(8,128)(2,1)}, bf16[1024,640]{1,0:T(8,128)(2,1)}, u32[]{:S(2)}, u32[]{:S(2)}) collective-permute-start(bf16[1024,640]{1,0:T(8,128)(2,1)} %param.16), channel_id=1, source_target_pairs={{0,3},{1,0},{2,1},{3,2},{4,7},{5,4},{6,5},{7,6},{8,11},{9,8},{10,9... | collective-permute-start | bytes 3932168 | tf_op jit(solution)/shard_map/ppermute | solution.py:200
  18.9 2.7 %copy-start.7 = (bf16[1024,640]{1,0:T(8,128)(2,1)S(1)}, bf16[1024,640]{1,0:T(8,128)(2,1)}, u32[]{:S(2)}) copy-start(bf16[1024,640]{1,0:T(8,128)(2,1)} %param.16) | copy-start | bytes 3932164
  18.9 3.9 %copy-start.1 = (bf16[1024,256]{1,0:T(8,128)(2,1)S(1)}, bf16[1024,256]{1,0:T(8,128)(2,1)}, u32[]{:S(2)}) copy-start(bf16[1024,256]{1,0:T(8,128)(2,1)} %k_ref.5) | copy-start | bytes 1572868
  18.9 3.9 %copy-start.3 = (bf16[1024,256]{1,0:T(8,128)(2,1)S(1)}, bf16[1024,256]{1,0:T(8,128)(2,1)}, u32[]{:S(2)}) copy-start(bf16[1024,256]{1,0:T(8,128)(2,1)} %v_ref.5) | copy-start | bytes 1572868
  56.2 26.1 %copy-start.8 = (s32[1024]{0:T(1024)S(1)}, s32[1024]{0:T(1024)}, u32[]{:S(2)}) copy-start(s32[1024]{0:T(1024)} %param.19) | copy-start | bytes 12292
  82.3 5.9 %copy-start.5 = (bf16[1024,1280]{1,0:T(8,128)(2,1)S(1)}, bf16[1024,1280]{1,0:T(8,128)(2,1)}, u32[]{:S(2)}) copy-start(bf16[1024,1280]{1,0:T(8,128)(2,1)} %get-tuple-element.58.o_ref) | copy-start | bytes 7864324
  85.9 2.3 copy-start.6
  97.2 145.4 %all-gather.5.cloned.1.call-start = ((), (), s32[]{:S(2)}) async-start(), calls=%async_computation.3 | async-start | bytes 6758400 | tf_op jit(solution)/shard_map/all_gather | solution.py:241
  185.1 11.9 %copy-start.2 = (bf16[1024,256]{1,0:T(8,128)(2,1)S(1)}, bf16[1024,256]{1,0:T(8,128)(2,1)}, u32[]{:S(2)}) copy-start(bf16[1024,256]{1,0:T(8,128)(2,1)} %k_ref.5) | copy-start | bytes 1572868
  185.1 11.9 %copy-start.4 = (bf16[1024,256]{1,0:T(8,128)(2,1)S(1)}, bf16[1024,256]{1,0:T(8,128)(2,1)}, u32[]{:S(2)}) copy-start(bf16[1024,256]{1,0:T(8,128)(2,1)} %v_ref.5) | copy-start | bytes 1572868
Sparse Core Ops, SparseCore 0:
  12.0 52.9 all-gather.2
  97.3 87.7 reduce-scatter.1
  187.3 48.7 all-gather.4
where the time goes:
time: 256 us; the launch traced here: 255 us
  waiting for transfers between devices  106 us (41%)
  Pallas kernels  73.6 us (29%)
  local copies, waits for them, and re-layouts  22.2 us (9%)
  matrix products  20.9 us (8%)
  between operations  13.9 us (5%)
  other arithmetic  11.6 us (5%)
  starting transfers between devices  6.99 us (3%)
    reduce_scatter x1, waiting for transfers between devices, layer(): lax.psum_scatter(local_term.astype(jnp.bfloat16), 'dp', scatter_dimension...  87.6 us
    pallas_call x2, Pallas kernels, attention_backward_group(): pl.pallas_call(functools.partial(backward_kernel, factor), grid=(1,), in_...  42.8 us
    pallas_call x1, Pallas kernels, attention_forward(): pl.pallas_call(functools.partial(forward_kernel, factor), grid=(groups,),...  30.8 us
    ppermute x3, waiting for transfers between devices, gather_features(): arrived.append(lax.ppermute(block, 'tensor', pairs))  18.3 us
    dot_general x1, matrix products, layer(): lax.dot_general(weighted, full_weight, (((1,), (1,)), ((), ())), preferre...  11.9 us
    dot_general x1, matrix products, layer(): lax.dot_general(attention_result, weighted, (((0,), (0,)), ((), ())), pre...  8.97 us
    dynamic_update_slice x4, local copies, waits for them, and re-layouts, gather_features(): full = lax.dynamic_update_slice(full, part, (0, source * width))  8.73 us
    unnamed x19, local copies, waits for them, and re-layouts  8.42 us
  transfers between devices with their start and end apart: 6, of which 2 were waited for; matrix products, arithmetic and copies ran while one was open for 10% of the time, Pallas kernels for 29%

commit v1 on v0

--- a/solution.py
+++ b/solution.py
@@ -194,14 +194,17 @@
 def gather_features(block):
     tensor_size = lax.axis_size("tensor")
     me = lax.axis_index("tensor")
-    arrived = [block]
+    arrived = [(me, block)]
     for shift in range(1, tensor_size):
         pairs = [(index, (index + shift) % tensor_size) for index in range(tensor_size)]
-        arrived.append(lax.ppermute(block, "tensor", pairs))
-    width = block.shape[1]
-    full = jnp.zeros((block.shape[0], tensor_size * width), block.dtype)
-    for shift, part in enumerate(arrived):
-        source = (me - shift) % tensor_size
+        moved = lax.ppermute(block, "tensor", pairs)
+        arrived.append(((me - shift) % tensor_size, moved))
+    return arrived
+
+
+def place_blocks(blocks, width):
+    full = jnp.zeros((blocks[0][1].shape[0], len(blocks) * width), blocks[0][1].dtype)
+    for source, part in blocks:
         full = lax.dynamic_update_slice(full, part, (0, source * width))
     return full
 
@@ -230,16 +233,26 @@
     token_weight = jnp.where(
         counted, jnp.sum(jnp.where(lang_match, lang_weight[None, :], 0.0), axis=1), 0.0
     )
-    full_grad = gather_features(loss_grad)
-    weighted = (token_weight[:, None] * full_grad.astype(jnp.float32)).astype(jnp.bfloat16)
-    local_term = lax.dot_general(
-        attention_result, weighted, (((0,), (0,)), ((), ())), preferred_element_type=jnp.float32
-    )
-    projection_part = lax.psum_scatter(
-        local_term.astype(jnp.bfloat16), "dp", scatter_dimension=0, tiled=True
-    )
-    projection_gradient = lax.all_gather(projection_part, "dp", axis=0, tiled=True)
-    local_term, weighted = lax.optimization_barrier((local_term, weighted))
+    width = loss_grad.shape[1]
+    weighted_blocks = [
+        (source, (token_weight[:, None] * part.astype(jnp.float32)).astype(jnp.bfloat16))
+        for source, part in gather_features(loss_grad)
+    ]
+    scattered = []
+    for source, part in weighted_blocks:
+        local_term = lax.dot_general(
+            attention_result, part, (((0,), (0,)), ((), ())), preferred_element_type=jnp.float32
+        )
+        scattered.append(
+            (
+                source,
+                lax.psum_scatter(
+                    local_term.astype(jnp.bfloat16), "dp", scatter_dimension=0, tiled=True
+                ),
+            )
+        )
+    projection_gradient = lax.all_gather(place_blocks(scattered, width), "dp", axis=0, tiled=True)
+    weighted = place_blocks(weighted_blocks, width)
     out_grad = lax.dot_general(
         weighted,
         full_weight,

time: 256 us -> 458 us (1.79)
  waiting for transfers between devices: 106 us -> 306 us
  matrix products: 20.9 us -> 25.9 us
    unnamed x3 -> x10, waiting for transfers between devices: 0.05 us -> 199 us
    reduce_scatter x1 -> x0, waiting for transfers between devices: 87.6 us -> none  [layer(): lax.psum_scatter(local_term.astype(jnp.bfloat16), 'dp', scatter_dimension...]
    ppermute x3, waiting for transfers between devices: 18.3 us -> 88.3 us  [gather_features(): moved = lax.ppermute(block, 'tensor', pairs)]
    all_gather x1, waiting for transfers between devices: 0.01 us -> 18.2 us  [layer(): lax.all_gather(attach_counts(out_weight, local_counts), 'dp', axis=1, til...]
    unnamed x19 -> x35, local copies, waits for them, and re-layouts: 8.42 us -> 16.4 us
    dot_general x1 -> x4, matrix products: 8.97 us -> 14.5 us  [layer(): lax.dot_general(attention_result, part, (((0,), (0,)), ((), ())), preferr...]
    dynamic_update_slice x4, local copies, waits for them, and re-layouts: 8.73 us -> 3.27 us  [place_blocks(): full = lax.dynamic_update_slice(full, part, (0, source * width))]
  transfers between devices with their start and end apart: 6 -> 9, of which waited for: 2 -> 7; matrix products, arithmetic and copies ran while one was open for 10% -> 6% of each run, Pallas kernels for 29% -> 16%
where the time goes in v1:
time: 458 us; the launch traced here: 457 us
  waiting for transfers between devices  306 us (67%)
  Pallas kernels  73.6 us (16%)
  matrix products  25.9 us (6%)
  local copies, waits for them, and re-layouts  22.5 us (5%)
  between operations  14.4 us (3%)
  other arithmetic  9.34 us (2%)
  starting transfers between devices  5.91 us (1%)
    unnamed x10, waiting for transfers between devices  199 us
    ppermute x3, waiting for transfers between devices, gather_features(): moved = lax.ppermute(block, 'tensor', pairs)  88.3 us
    pallas_call x2, Pallas kernels, attention_backward_group(): pl.pallas_call(functools.partial(backward_kernel, factor), grid=(1,), in_...  42.9 us
    pallas_call x1, Pallas kernels, attention_forward(): pl.pallas_call(functools.partial(forward_kernel, factor), grid=(groups,),...  30.7 us
    all_gather x1, waiting for transfers between devices, layer(): lax.all_gather(attach_counts(out_weight, local_counts), 'dp', axis=1, til...  18.2 us
    unnamed x35, local copies, waits for them, and re-layouts  16.4 us
    dot_general x4, matrix products, layer(): lax.dot_general(attention_result, part, (((0,), (0,)), ((), ())), preferr...  14.5 us
    dot_general x1, matrix products, layer(): lax.dot_general(weighted, full_weight, (((1,), (1,)), ((), ())), preferre...  11.4 us
  transfers between devices with their start and end apart: 9, of which 7 were waited for; matrix products, arithmetic and copies ran while one was open for 6% of the time, Pallas kernels for 16%

profile of v1, /device:TPU:0, one launch (start us, length us, event | category | flops | bytes accessed | tf_op | source)
XLA Modules:
  0.0 457.5 jit_solution(15761000885531356947)
XLA Ops:
  10.1 1.6 pad_maximum_fusion.3
  12.0 1.7 copy-done
  15.8 30.7 %shard_map.119 = (bf16[1024,1280]{1,0:T(8,128)(2,1)}, f32[2,5,1024,128]{3,2,1,0:T(8,128)}) custom-call(bf16[1024,1280]{1,0:T(8,128)(2,1)S(1)} %copy-done, bf16[1024,256]{1,0:T(8,128)(2,1)S(1)} %copy-done.2, bf16[1024,256]{1,0:T(8,128)(2,1)S(1)} %copy-done.4, s32[1024,1]{1,0:T(8,128)S(1)} %copy.26.row_doc_ref, s32[1,1024]{1,0:T(1,128)S(1)} %bitcast.30), custom_call_target="tpu_custom_call" | custom-call | flops 2684354560 | bytes 17825792 | tf_op jit(solution)/shard_map/pallas_call | solution.py:119
  46.6 18.2 %all-gather.3.cloned.1.call-done = bf16[1296,2560]{0,1:T(8,128)(2,1)} async-done(((bf16[1296,80]{0,1:T(8,128)(2,1)}), bf16[1296,2560]{0,1:T(8,128)(2,1)}) %all-gather.3.cloned.1.call-update) | async-done | bytes 6635536 | tf_op jit(solution)/shard_map/all_gather | solution.py:227
  64.8 1.2 slice.54
  67.7 3.6 convolution_convert_fusion.3
  71.4 1.7 collective-permute-start
  73.0 30.8 %collective-permute-done = bf16[1024,640]{1,0:T(8,128)(2,1)S(1)} collective-permute-done((bf16[1024,640]{1,0:T(8,128)(2,1)}, bf16[1024,640]{1,0:T(8,128)(2,1)S(1)}, u32[]{:S(2)}, u32[]{:S(2)}) %collective-permute-start) | collective-permute-done | bytes 1310752 | tf_op jit(solution)/shard_map/ppermute | solution.py:200
  104.8 3.7 convolution_convert_fusion.2
  108.6 2.0 collective-permute-start.1
  110.6 29.8 %collective-permute-done.1 = bf16[1024,640]{1,0:T(8,128)(2,1)S(1)} collective-permute-done((bf16[1024,640]{1,0:T(8,128)(2,1)}, bf16[1024,640]{1,0:T(8,128)(2,1)S(1)}, u32[]{:S(2)}, u32[]{:S(2)}) %collective-permute-start.1) | collective-permute-done | bytes 1310752 | tf_op jit(solution)/shard_map/ppermute | solution.py:200
  141.5 3.6 convolution_convert_fusion.1
  145.2 2.0 collective-permute-start.2
  147.2 27.7 %collective-permute-done.2 = bf16[1024,640]{1,0:T(8,128)(2,1)S(1)} collective-permute-done((bf16[1024,640]{1,0:T(8,128)(2,1)}, bf16[1024,640]{1,0:T(8,128)(2,1)S(1)}, u32[]{:S(2)}, u32[]{:S(2)}) %collective-permute-start.2) | collective-permute-done | bytes 1310752 | tf_op jit(solution)/shard_map/ppermute | solution.py:200
  175.9 3.6 convolution_convert_fusion
  180.6 44.0 %reduce-scatter.15.cloned.1.call-done = bf16[40,640]{1,0:T(8,128)(2,1)} async-done(((bf16[1280,640]{1,0:T(8,128)(2,1)}), bf16[40,640]{1,0:T(8,128)(2,1)}) %reduce-scatter.15.cloned.1.call-update) | async-done | bytes 51216
  225.4 77.6 %reduce-scatter.17.cloned.1.call-done = bf16[40,640]{1,0:T(8,128)(2,1)} async-done(((bf16[1280,640]{1,0:T(8,128)(2,1)}), bf16[40,640]{1,0:T(8,128)(2,1)}) %reduce-scatter.17.cloned.1.call-update) | async-done | bytes 51216
  303.8 77.6 %reduce-scatter.19.cloned.1.call-done = bf16[40,640]{1,0:T(8,128)(2,1)} async-done(((bf16[1280,640]{1,0:T(8,128)(2,1)}), bf16[40,640]{1,0:T(8,128)(2,1)}) %reduce-scatter.19.cloned.1.call-update) | async-done | bytes 51216
  387.4 11.4 %fusion.2.do_ref = bf16[1024,1280]{1,0:T(8,128)(2,1)} fusion(bf16[1024,2560]{1,0:T(8,128)(2,1)S(1)} %fusion.8, bf16[1296,2560]{0,1:T(8,128)(2,1)} %all-gather.3.cloned.1.call-done), kind=kOutput, calls=%fused_computation.2 | convolution fusion | flops 6712197120 | bytes 14417920 | tf_op jit(solution)/shard_map/dot_general | solution.py:256
  398.8 21.3 %shard_map.121 = (bf16[1024,640]{1,0:T(8,128)(2,1)S(1)}, bf16[1024,128]{1,0:T(8,128)(2,1)S(1)}, bf16[1024,128]{1,0:T(8,128)(2,1)S(1)}) custom-call(bf16[1024,1280]{1,0:T(8,128)(2,1)S(1)} %copy-done.1, bf16[1024,256]{1,0:T(8,128)(2,1)S(1)} %copy-done.3, bf16[1024,256]{1,0:T(8,128)(2,1)S(1)} %copy-done.5, s32[1024,1]{1,0:T(8,128)S(1)} %copy.26.row_doc_ref, ...), custom_call_target="tpu_custom_call" | custom-call | flops 3355443200 | bytes 9961472 | tf_op jit(solution)/shard_map/pallas_call | solution.py:150
  420.2 21.6 %shard_map.120 = (bf16[1024,640]{1,0:T(8,128)(2,1)S(1)}, bf16[1024,128]{1,0:T(8,128)(2,1)S(1)}, bf16[1024,128]{1,0:T(8,128)(2,1)S(1)}) custom-call(bf16[1024,1280]{1,0:T(8,128)(2,1)S(1)} %copy-done.1, bf16[1024,256]{1,0:T(8,128)(2,1)S(1)} %copy-done.3, bf16[1024,256]{1,0:T(8,128)(2,1)S(1)} %copy-done.5, s32[1024,1]{1,0:T(8,128)S(1)} %copy.26.row_doc_ref, ...), custom_call_target="tpu_custom_call" | custom-call | flops 3355443200 | bytes 9961472 | tf_op jit(solution)/shard_map/pallas_call | solution.py:150
  441.8 1.1 pad_maximum_fusion.1
  442.9 1.7 pad_maximum_fusion
  444.5 6.1 %copy.40 = bf16[1280,2560]{1,0:T(8,128)(2,1)} copy(bf16[1280,2560]{1,0:T(8,128)(2,1)} %all-gather.5.cloned.1.call-done) | data formatting | bytes 13107200
  (74 shorter events, 18.8 us)
Async XLA Ops:
  7.2 57.6 %all-gather.3.cloned.1.call-start = ((), (), s32[]{:S(2)}) async-start(), calls=%async_computation.4 | async-start | bytes 7434240 | tf_op jit(solution)/shard_map/all_gather | solution.py:227
  11.7 168.0 %reduce-scatter.13.cloned.1.call-start = ((), (), s32[]{:S(2)}) async-start(), calls=%async_computation.6 | async-start | bytes 1689600
  12.0 1.7 copy-start
  13.8 1.0 copy-start.2
  46.6 21.1 %copy-start.16 = (s32[1024]{0:T(1024)S(1)}, s32[1024]{0:T(1024)}, u32[]{:S(2)}) copy-start(s32[1024]{0:T(1024)} %param.19) | copy-start | bytes 12292
  46.6 21.1 %copy-start.6 = (bf16[1024,1280]{1,0:T(8,128)(2,1)S(1)}, bf16[1024,1280]{1,0:T(8,128)(2,1)}, u32[]{:S(2)}) copy-start(bf16[1024,1280]{1,0:T(8,128)(2,1)} %get-tuple-element.56.o_ref) | copy-start | bytes 7864324
  64.8 2.9 copy-start.7
  71.3 153.3 %reduce-scatter.15.cloned.1.call-start = ((), (), s32[]{:S(2)}) async-start(), calls=%async_computation.7 | async-start | bytes 1689600
  71.4 32.4 %collective-permute-start = (bf16[1024,640]{1,0:T(8,128)(2,1)}, bf16[1024,640]{1,0:T(8,128)(2,1)S(1)}, u32[]{:S(2)}, u32[]{:S(2)}) collective-permute-start(bf16[1024,640]{1,0:T(8,128)(2,1)} %param.16), channel_id=1, source_target_pairs={{0,1},{1,2},{2,3},{3,0},{4,5},{5,6},{6,7},{7,4},{8,9},{9,10},{10,1... | collective-permute-start | bytes 3932168 | tf_op jit(solution)/shard_map/ppermute | solution.py:200
  103.8 1.1 copy-start.9
  108.5 194.5 %reduce-scatter.17.cloned.1.call-start = ((), (), s32[]{:S(2)}) async-start(), calls=%async_computation.8 | async-start | bytes 1689600
  108.6 31.9 %collective-permute-start.1 = (bf16[1024,640]{1,0:T(8,128)(2,1)}, bf16[1024,640]{1,0:T(8,128)(2,1)S(1)}, u32[]{:S(2)}, u32[]{:S(2)}) collective-permute-start(bf16[1024,640]{1,0:T(8,128)(2,1)} %param.16), channel_id=1, source_target_pairs={{0,2},{1,3},{2,0},{3,1},{4,6},{5,7},{6,4},{7,5},{8,10},{9,11},{10,... | collective-permute-start | bytes 3932168 | tf_op jit(solution)/shard_map/ppermute | solution.py:200
  140.4 1.1 copy-start.11
  145.2 236.3 %reduce-scatter.19.cloned.1.call-start = ((), (), s32[]{:S(2)}) async-start(), calls=%async_computation.9 | async-start | bytes 1689600
  145.2 29.7 %collective-permute-start.2 = (bf16[1024,640]{1,0:T(8,128)(2,1)}, bf16[1024,640]{1,0:T(8,128)(2,1)S(1)}, u32[]{:S(2)}, u32[]{:S(2)}) collective-permute-start(bf16[1024,640]{1,0:T(8,128)(2,1)} %param.16), channel_id=1, source_target_pairs={{0,3},{1,0},{2,1},{3,2},{4,7},{5,4},{6,5},{7,6},{8,11},{9,8},{10,9... | collective-permute-start | bytes 3932168 | tf_op jit(solution)/shard_map/ppermute | solution.py:200
  174.9 1.1 copy-start.13
  179.6 265.0 %all-gather.5.cloned.1.call-start = ((), (), s32[]{:S(2)}) async-start(), calls=%async_computation.5 | async-start | bytes 6758400 | tf_op jit(solution)/shard_map/all_gather | solution.py:254
  383.0 1.3 copy-start.8
  384.3 1.3 copy-start.10
  384.3 1.7 copy-start.12
  385.6 1.4 copy-start.14
  387.4 11.4 %copy-start.1 = (bf16[1024,1280]{1,0:T(8,128)(2,1)S(1)}, bf16[1024,1280]{1,0:T(8,128)(2,1)}, u32[]{:S(2)}) copy-start(bf16[1024,1280]{1,0:T(8,128)(2,1)} %q_ref.5) | copy-start | bytes 7864324
  387.4 11.4 %copy-start.3 = (bf16[1024,256]{1,0:T(8,128)(2,1)S(1)}, bf16[1024,256]{1,0:T(8,128)(2,1)}, u32[]{:S(2)}) copy-start(bf16[1024,256]{1,0:T(8,128)(2,1)} %k_ref.5) | copy-start | bytes 1572868
  387.4 11.4 %copy-start.5 = (bf16[1024,256]{1,0:T(8,128)(2,1)S(1)}, bf16[1024,256]{1,0:T(8,128)(2,1)}, u32[]{:S(2)}) copy-start(bf16[1024,256]{1,0:T(8,128)(2,1)} %v_ref.5) | copy-start | bytes 1572868
  (2 other events, 1.7 us)
Sparse Core Ops, SparseCore 0:
  11.8 52.8 all-gather.2
  71.4 74.5 reduce-scatter.12
  149.7 74.7 reduce-scatter.14
  228.2 74.8 reduce-scatter.16
  306.6 74.7 reduce-scatter.18
  383.6 48.6 all-gather.4

commit v2 on v0

--- a/solution.py
+++ b/solution.py
@@ -15,6 +15,7 @@
 LANGS = 29
 DOCS = 16
 COUNT_BASE = 32
+DP_AXES = ("dp_x", "dp_y", "dp_core")
 
 
 def token_docs(length_row, row_count):
@@ -221,10 +222,10 @@
     lang_match = token_lang[:, None] == jnp.arange(LANGS, dtype=jnp.int32)[None, :]
     local_counts = jnp.sum((lang_match & counted[:, None]).astype(jnp.int32), axis=0)
     weight_rows = out_weight.shape[0]
-    gathered = lax.all_gather(attach_counts(out_weight, local_counts), "dp", axis=1, tiled=True)
+    gathered = lax.all_gather(attach_counts(out_weight, local_counts), DP_AXES, axis=1, tiled=True)
     full_weight = gathered[:weight_rows]
     code = gathered[weight_rows : weight_rows + 2].astype(jnp.float32)
-    code = code.reshape(2, lax.axis_size("dp"), out_weight.shape[1])[:, :, :LANGS]
+    code = code.reshape(2, lax.axis_size(DP_AXES), out_weight.shape[1])[:, :, :LANGS]
     counts = jnp.sum(code[0] * COUNT_BASE + code[1], axis=0)
     lang_weight = jnp.sqrt(jnp.sum(counts) / (LANGS * jnp.maximum(counts, 1.0)))
     token_weight = jnp.where(
@@ -235,10 +236,14 @@
     local_term = lax.dot_general(
         attention_result, weighted, (((0,), (0,)), ((), ())), preferred_element_type=jnp.float32
     )
-    projection_part = lax.psum_scatter(
-        local_term.astype(jnp.bfloat16), "dp", scatter_dimension=0, tiled=True
-    )
-    projection_gradient = lax.all_gather(projection_part, "dp", axis=0, tiled=True)
+    projection_part = local_term.astype(jnp.bfloat16)
+    for axis in reversed(DP_AXES):
+        projection_part = lax.psum_scatter(
+            projection_part, axis, scatter_dimension=0, tiled=True
+        )
+    projection_gradient = projection_part
+    for axis in DP_AXES:
+        projection_gradient = lax.all_gather(projection_gradient, axis, axis=0, tiled=True)
     local_term, weighted = lax.optimization_barrier((local_term, weighted))
     out_grad = lax.dot_general(
         weighted,
@@ -250,9 +255,7 @@
     parts = []
     for group in range(keys.shape[1] // HEAD_SIZE):
         parts.append(
-            attention_backward_group(
-                group, query, keys, values, doc_ids, attention_result, out_grad, log_rows, factor
-            )
+            attention_backward_group(group, query, keys, values, doc_ids, attention_result, out_grad, log_rows, factor)
         )
     query_gradient, key_gradient, value_gradient = (
         jnp.concatenate([part[k] for part in parts], axis=1) for k in range(3)
@@ -262,20 +265,24 @@
 
 def solution(mesh):
     in_specs = (
-        P("dp", "tensor"),
-        P("dp", "tensor"),
-        P("dp", "tensor"),
-        P("tensor", "dp"),
-        P("dp", "tensor"),
-        P("dp", None),
-        P("dp", None),
-        P("dp"),
+        P(DP_AXES, "tensor"),
+        P(DP_AXES, "tensor"),
+        P(DP_AXES, "tensor"),
+        P("tensor", DP_AXES),
+        P(DP_AXES, "tensor"),
+        P(DP_AXES, None),
+        P(DP_AXES, None),
+        P(DP_AXES),
     )
     out_specs = (
-        P("dp", "tensor"),
-        P("dp", "tensor"),
-        P("dp", "tensor"),
-        P("dp", "tensor"),
+        P(DP_AXES, "tensor"),
+        P(DP_AXES, "tensor"),
+        P(DP_AXES, "tensor"),
+        P(DP_AXES, "tensor"),
         P("tensor", None),
     )
-    return jax.shard_map(layer, mesh=mesh, in_specs=in_specs, out_specs=out_specs, check_vma=False)
+    dp = mesh.shape["dp"]
+    split_mesh = jax.sharding.Mesh(
+        mesh.devices.reshape(dp // 8, 4, 2, mesh.shape["tensor"]), DP_AXES + ("tensor",)
+    )
+    return jax.shard_map(layer, mesh=split_mesh, in_specs=in_specs, out_specs=out_specs, check_vma=False)

time: 256 us -> 313 us (1.22)
  waiting for transfers between devices: 106 us -> 146 us
  blocking collectives: 0 us -> 15 us
    all_gather x2 -> x3, waiting for transfers between devices: 0.01 us -> 40.7 us  [the longest x2 40.7 us: layer(): lax.all_gather(projection_gradient, axis, axis=0, tiled=True)]
    all_gather x0 -> x1, blocking collectives: none -> 15 us  [layer(): lax.all_gather(projection_gradient, axis, axis=0, tiled=True)]
    reduce_scatter x1 -> x3, waiting for transfers between devices: 87.6 us -> 87 us  [layer(): lax.psum_scatter(projection_part, axis, scatter_dimension=0, tiled=True)]
  transfers between devices with their start and end apart: 6 -> 9, of which waited for: 2 -> 5; matrix products, arithmetic and copies ran while one was open for 10% -> 8% of each run, Pallas kernels for 29% -> 24%
where the time goes in v2:
time: 313 us; the launch traced here: 312 us
  waiting for transfers between devices  146 us (47%)
  Pallas kernels  74.4 us (24%)
  local copies, waits for them, and re-layouts  22.2 us (7%)
  matrix products  20.9 us (7%)
  blocking collectives  15 us (5%)
  between operations  14.3 us (5%)
  other arithmetic  11.6 us (4%)
  starting transfers between devices  7.11 us (2%)
    reduce_scatter x3, waiting for transfers between devices, layer(): lax.psum_scatter(projection_part, axis, scatter_dimension=0, tiled=True)  87 us
    pallas_call x2, Pallas kernels, attention_backward_group(): pl.pallas_call(functools.partial(backward_kernel, factor), grid=(1,), in_...  43.7 us
    all_gather x2, waiting for transfers between devices, layer(): lax.all_gather(projection_gradient, axis, axis=0, tiled=True)  40.7 us
    pallas_call x1, Pallas kernels, attention_forward(): pl.pallas_call(functools.partial(forward_kernel, factor), grid=(groups,),...  30.8 us
    ppermute x3, waiting for transfers between devices, gather_features(): arrived.append(lax.ppermute(block, 'tensor', pairs))  18.4 us
    all_gather x1, blocking collectives, layer(): lax.all_gather(projection_gradient, axis, axis=0, tiled=True)  15 us
    dot_general x1, matrix products, layer(): lax.dot_general(weighted, full_weight, (((1,), (1,)), ((), ())), preferre...  11.9 us
    dot_general x1, matrix products, layer(): lax.dot_general(attention_result, weighted, (((0,), (0,)), ((), ())), pre...  8.97 us
  transfers between devices with their start and end apart: 9, of which 5 were waited for; matrix products, arithmetic and copies ran while one was open for 8% of the time, Pallas kernels for 24%

profile of v2, /device:TPU:0, one launch (start us, length us, event | category | flops | bytes accessed | tf_op | source)
XLA Modules:
  0.0 311.7 jit_solution(2189027160880358166)
XLA Ops:
  10.2 1.6 pad_maximum_fusion.3
  11.9 2.1 collective-permute-start
  14.0 3.6 %collective-permute-start.1 = (bf16[1024,640]{1,0:T(8,128)(2,1)}, bf16[1024,640]{1,0:T(8,128)(2,1)}, u32[]{:S(2)}, u32[]{:S(2)}) collective-permute-start(bf16[1024,640]{1,0:T(8,128)(2,1)} %param.16), channel_id=1, source_target_pairs={{0,2},{1,3},{2,0},{3,1},{4,6},{5,7},{6,4},{7,5},{8,10},{9,11},{10,... | collective-permute-start | bytes 3932168 | tf_op jit(solution)/shard_map/ppermute | solution.py:201
  18.9 2.7 broadcast_in_dim.61
  21.6 1.2 constant_dynamic-update-slice_fusion.3
  22.8 30.8 %shard_map.119 = (bf16[1024,1280]{1,0:T(8,128)(2,1)}, f32[2,5,1024,128]{3,2,1,0:T(8,128)}) custom-call(bf16[1024,1280]{1,0:T(8,128)(2,1)S(1)} %copy-done, bf16[1024,256]{1,0:T(8,128)(2,1)S(1)} %copy-done.1, bf16[1024,256]{1,0:T(8,128)(2,1)S(1)} %copy-done.3, s32[1024,1]{1,0:T(8,128)S(1)} %copy.21.row_doc_ref, s32[1,1024]{1,0:T(1,128)S(1)} %bitcast.27), custom_call_target="tpu_custom_call" | custom-call | flops 2684354560 | bytes 17825792 | tf_op jit(solution)/shard_map/pallas_call | solution.py:120
  53.6 2.6 constant_dynamic-update-slice_fusion.2
  56.2 18.3 %collective-permute-done.1 = bf16[1024,640]{1,0:T(8,128)(2,1)} collective-permute-done((bf16[1024,640]{1,0:T(8,128)(2,1)}, bf16[1024,640]{1,0:T(8,128)(2,1)}, u32[]{:S(2)}, u32[]{:S(2)}) %collective-permute-start.1) | collective-permute-done | bytes 1310752 | tf_op jit(solution)/shard_map/ppermute | solution.py:201
  74.5 2.5 constant_dynamic-update-slice_fusion.1
  77.0 2.5 constant_dynamic-update-slice_fusion
  79.5 1.1 slice.54
  82.3 3.5 %multiply_convert_fusion = bf16[1024,2560]{1,0:T(8,128)(2,1)S(1)} fusion(bf16[1024,2560]{1,0:T(8,128)(2,1)} %constant_dynamic-update-slice_fusion, f32[1024]{0:T(1024)S(1)} %broadcast_select_fusion), kind=kLoop, calls=%fused_computation | loop fusion | flops 7864320 | bytes 10489856 | tf_op jit(solution)/shard_map/convert_element_type | solution.py:235
  85.9 2.3 copy-done.6
  88.2 9.0 %fusion.10 = bf16[1280,2560]{1,0:T(8,128)(2,1)} fusion(bf16[1024,1280]{1,0:T(8,128)(2,1)S(1)} %copy-done.5, bf16[1024,2560]{1,0:T(8,128)(2,1)S(1)} %multiply_convert_fusion), kind=kOutput, calls=%fused_computation.35 | convolution fusion | flops 6710886400 | bytes 14417920 | tf_op jit(solution)/shard_map/dot_general | solution.py:236
  97.2 19.3 %reduce-scatter.4.cloned.1.call-done = bf16[640,2560]{1,0:T(8,128)(2,1)} async-done(((bf16[1280,2560]{1,0:T(8,128)(2,1)}), bf16[640,2560]{1,0:T(8,128)(2,1)}) %reduce-scatter.4.cloned.1.call-update) | async-done | bytes 3276816 | tf_op jit(solution)/shard_map/reduce_scatter | solution.py:241
  116.6 43.1 %reduce-scatter.6.cloned.1.call-done = bf16[160,2560]{1,0:T(8,128)(2,1)} async-done(((bf16[640,2560]{1,0:T(8,128)(2,1)}), bf16[160,2560]{1,0:T(8,128)(2,1)}) %reduce-scatter.6.cloned.1.call-update) | async-done | bytes 819216 | tf_op jit(solution)/shard_map/reduce_scatter | solution.py:241
  159.8 24.6 %reduce-scatter.8.cloned.1.call-done = bf16[40,2560]{1,0:T(8,128)(2,1)} async-done(((bf16[160,2560]{1,0:T(8,128)(2,1)}), bf16[40,2560]{1,0:T(8,128)(2,1)}) %reduce-scatter.8.cloned.1.call-update) | async-done | bytes 204816 | tf_op jit(solution)/shard_map/reduce_scatter | solution.py:241
  184.4 15.0 %all_gather.13 = bf16[160,2560]{1,0:T(8,128)(2,1)} all-gather(bf16[40,2560]{1,0:T(8,128)(2,1)} %reduce-scatter.8.cloned.1.call-done), channel_id=1, replica_groups=mesh['dp_x'=4,'dp_y'=4,'dp_core'=2,'tensor'=4] {'dp_x'}, dimensions={0}, use_global_device_ids=true | all-gather | bytes 1024000 | tf_op jit(solution)/shard_map/all_gather | solution.py:246
  199.6 40.7 %all-gather.6.cloned.1.call-done = bf16[640,2560]{1,0:T(8,128)(2,1)} async-done(((bf16[160,2560]{1,0:T(8,128)(2,1)}), bf16[640,2560]{1,0:T(8,128)(2,1)}) %all-gather.6.cloned.1.call-update) | async-done | bytes 3276816 | tf_op jit(solution)/shard_map/all_gather | solution.py:246
  240.4 11.9 %fusion.2.do_ref = bf16[1024,1280]{1,0:T(8,128)(2,1)} fusion(bf16[1024,2560]{1,0:T(8,128)(2,1)} %copy-done.6, bf16[1296,2560]{0,1:T(8,128)(2,1)} %all-gather.4.cloned.1.call-done), kind=kOutput, calls=%fused_computation.3 | convolution fusion | flops 6712197120 | bytes 14417920 | tf_op jit(solution)/shard_map/dot_general | solution.py:248
  252.3 22.3 %shard_map.121 = (bf16[1024,640]{1,0:T(8,128)(2,1)S(1)}, bf16[1024,128]{1,0:T(8,128)(2,1)S(1)}, bf16[1024,128]{1,0:T(8,128)(2,1)S(1)}) custom-call(bf16[1024,1280]{1,0:T(8,128)(2,1)S(1)} %copy-done, bf16[1024,256]{1,0:T(8,128)(2,1)S(1)} %copy-done.2, bf16[1024,256]{1,0:T(8,128)(2,1)S(1)} %copy-done.4, s32[1024,1]{1,0:T(8,128)S(1)} %copy.21.row_doc_ref, ...), custom_call_target="tpu_custom_call" | custom-call | flops 3355443200 | bytes 9961472 | tf_op jit(solution)/shard_map/pallas_call | solution.py:151
  274.6 21.4 %shard_map.120 = (bf16[1024,640]{1,0:T(8,128)(2,1)S(1)}, bf16[1024,128]{1,0:T(8,128)(2,1)S(1)}, bf16[1024,128]{1,0:T(8,128)(2,1)S(1)}) custom-call(bf16[1024,1280]{1,0:T(8,128)(2,1)S(1)} %copy-done, bf16[1024,256]{1,0:T(8,128)(2,1)S(1)} %copy-done.2, bf16[1024,256]{1,0:T(8,128)(2,1)S(1)} %copy-done.4, s32[1024,1]{1,0:T(8,128)S(1)} %copy.21.row_doc_ref, ...), custom_call_target="tpu_custom_call" | custom-call | flops 3355443200 | bytes 9961472 | tf_op jit(solution)/shard_map/pallas_call | solution.py:151
  297.1 1.7 pad_maximum_fusion
  298.7 6.1 %copy.31 = bf16[1280,2560]{1,0:T(8,128)(2,1)} copy(bf16[1280,2560]{1,0:T(8,128)(2,1)} %all-gather.8.cloned.1.call-done) | data formatting | bytes 13107200
  (52 shorter events, 7.5 us)
Async XLA Ops:
  7.2 15.6 %copy-start = (bf16[1024,1280]{1,0:T(8,128)(2,1)S(1)}, bf16[1024,1280]{1,0:T(8,128)(2,1)}, u32[]{:S(2)}) copy-start(bf16[1024,1280]{1,0:T(8,128)(2,1)} %q_ref.5) | copy-start | bytes 7864324
  7.2 72.3 %all-gather.4.cloned.1.call-start = ((), (), s32[]{:S(2)}) async-start(), calls=%async_computation.3 | async-start | bytes 7434240 | tf_op jit(solution)/shard_map/all_gather | solution.py:225
  11.9 104.6 %reduce-scatter.4.cloned.1.call-start = ((), (), s32[]{:S(2)}) async-start(), calls=%async_computation.4 | async-start | bytes 9830400 | tf_op jit(solution)/shard_map/reduce_scatter | solution.py:241
  11.9 41.6 %collective-permute-start = (bf16[1024,640]{1,0:T(8,128)(2,1)}, bf16[1024,640]{1,0:T(8,128)(2,1)}, u32[]{:S(2)}, u32[]{:S(2)}) collective-permute-start(bf16[1024,640]{1,0:T(8,128)(2,1)} %param.16), channel_id=1, source_target_pairs={{0,1},{1,2},{2,3},{3,0},{4,5},{5,6},{6,7},{7,4},{8,9},{9,10},{10,1... | collective-permute-start | bytes 3932168 | tf_op jit(solution)/shard_map/ppermute | solution.py:201
  14.0 60.5 %collective-permute-start.1 = (bf16[1024,640]{1,0:T(8,128)(2,1)}, bf16[1024,640]{1,0:T(8,128)(2,1)}, u32[]{:S(2)}, u32[]{:S(2)}) collective-permute-start(bf16[1024,640]{1,0:T(8,128)(2,1)} %param.16), channel_id=1, source_target_pairs={{0,2},{1,3},{2,0},{3,1},{4,6},{5,7},{6,4},{7,5},{8,10},{9,11},{10,... | collective-permute-start | bytes 3932168 | tf_op jit(solution)/shard_map/ppermute | solution.py:201
  17.6 59.4 %collective-permute-start.2 = (bf16[1024,640]{1,0:T(8,128)(2,1)}, bf16[1024,640]{1,0:T(8,128)(2,1)}, u32[]{:S(2)}, u32[]{:S(2)}) collective-permute-start(bf16[1024,640]{1,0:T(8,128)(2,1)} %param.16), channel_id=1, source_target_pairs={{0,3},{1,0},{2,1},{3,2},{4,7},{5,4},{6,5},{7,6},{8,11},{9,8},{10,9... | collective-permute-start | bytes 3932168 | tf_op jit(solution)/shard_map/ppermute | solution.py:201
  18.9 2.7 copy-start.7
  18.9 3.9 %copy-start.1 = (bf16[1024,256]{1,0:T(8,128)(2,1)S(1)}, bf16[1024,256]{1,0:T(8,128)(2,1)}, u32[]{:S(2)}) copy-start(bf16[1024,256]{1,0:T(8,128)(2,1)} %k_ref.5) | copy-start | bytes 1572868
  18.9 3.9 %copy-start.3 = (bf16[1024,256]{1,0:T(8,128)(2,1)S(1)}, bf16[1024,256]{1,0:T(8,128)(2,1)}, u32[]{:S(2)}) copy-start(bf16[1024,256]{1,0:T(8,128)(2,1)} %v_ref.5) | copy-start | bytes 1572868
  56.2 26.1 %copy-start.8 = (s32[1024]{0:T(1024)S(1)}, s32[1024]{0:T(1024)}, u32[]{:S(2)}) copy-start(s32[1024]{0:T(1024)} %param.19) | copy-start | bytes 12292
  82.3 5.9 %copy-start.5 = (bf16[1024,1280]{1,0:T(8,128)(2,1)S(1)}, bf16[1024,1280]{1,0:T(8,128)(2,1)}, u32[]{:S(2)}) copy-start(bf16[1024,1280]{1,0:T(8,128)(2,1)} %get-tuple-element.58.o_ref) | copy-start | bytes 7864324
  85.9 2.3 copy-start.6
  97.2 62.5 %reduce-scatter.6.cloned.1.call-start = ((), (), s32[]{:S(2)}) async-start(), calls=%async_computation.5 | async-start | bytes 4096000 | tf_op jit(solution)/shard_map/reduce_scatter | solution.py:241
  116.5 67.9 %reduce-scatter.8.cloned.1.call-start = ((), (), s32[]{:S(2)}) async-start(), calls=%async_computation.6 | async-start | bytes 1024000 | tf_op jit(solution)/shard_map/reduce_scatter | solution.py:241
  159.7 80.6 %all-gather.6.cloned.1.call-start = ((), (), s32[]{:S(2)}) async-start(), calls=%async_computation.7 | async-start | bytes 4096000 | tf_op jit(solution)/shard_map/all_gather | solution.py:246
  199.4 99.3 %all-gather.8.cloned.1.call-start = ((), (), s32[]{:S(2)}) async-start(), calls=%async_computation.8 | async-start | bytes 9830400 | tf_op jit(solution)/shard_map/all_gather | solution.py:246
  240.4 11.9 %copy-start.2 = (bf16[1024,256]{1,0:T(8,128)(2,1)S(1)}, bf16[1024,256]{1,0:T(8,128)(2,1)}, u32[]{:S(2)}) copy-start(bf16[1024,256]{1,0:T(8,128)(2,1)} %k_ref.5) | copy-start | bytes 1572868
  240.4 11.9 %copy-start.4 = (bf16[1024,256]{1,0:T(8,128)(2,1)S(1)}, bf16[1024,256]{1,0:T(8,128)(2,1)}, u32[]{:S(2)}) copy-start(bf16[1024,256]{1,0:T(8,128)(2,1)} %v_ref.5) | copy-start | bytes 1572868
Sparse Core Ops, SparseCore 0:
  12.0 52.9 all-gather.3
  97.3 19.1 reduce-scatter.3
  118.9 40.7 reduce-scatter.5
  162.0 22.3 reduce-scatter.7
  199.5 40.7 all-gather.5
  241.8 19.9 all-gather.7
